TPU v7x, 128 devices: a whole 4x4x4 slice. The times are simulated.
128 devices in a mesh: dp: 32 (over y, z, core), mp: 4 (over x).
Axes of the slice: x: 4, y: 4, z: 4, core: 2. Of those that a mesh axis runs over, the one named last changes fastest.
Arguments:
- hidden_rows: bfloat16 [16384, 4096], P('dp', 'mp'), may hold values from -3 to 3
- destination: int32 [16384], P('dp'), may hold values from 0 to 16383, as said below
- doc_ids: int32 [16384], P('dp'), may hold values from 0 to 63, never falling along the last dimension, each value on 1 to 8704 neighbouring positions
- norm_gain: float32 [4096], replicated, may hold values from 0.1 to 1.9
- w_query: bfloat16 [4096, 2048], P(None, 'mp'), may hold values from -1 to 1
- w_key: bfloat16 [4096, 512], P(None, 'mp'), may hold values from -1 to 1
- w_value: bfloat16 [4096, 512], P(None, 'mp'), may hold values from -0.09375 to 0.09375
- w_out: bfloat16 [2048, 4096], P('mp'), may hold values from -0.125 to 0.125
Outputs:
- layer_out: bfloat16 [16384, 4096], P('dp', 'mp')
Inputs may be any that keep to these rules, and one draw needn't show every extreme that they name: `destination`: A permutation of the rows. Each aligned block of 512 rows sends exactly 32 rows to each of half of the 512-row blocks of document order and none to the other half, and each block of document order receives exactly 32 rows from each of half of the blocks of token order.
All inputs are finite; a program needn't handle non-finite values.
Results may differ from a plain program's by a relative error of at most 0.011.
Values may be sent and summed in bfloat16 or wider, within the bound.
No kernel may reach another device: no remote copies, remote signals or barrier semaphores. Data moves between devices by JAX's collectives and lax.ppermute only.
A program may use at most 128 MiB of HBM per device.

v0:
```python
import math
import jax
import jax.numpy as jnp
from jax import lax
from jax.sharding import PartitionSpec as P

HD = 128
ROPE_BASE = 500000.0
NORM_EPS = 1e-05
NEG_START = -1e30
key_block = 512


def rope_angles(row_index):
    lane_index = jnp.arange(HD // 2, dtype=jnp.float32)
    frequency = jnp.power(jnp.float32(ROPE_BASE), -2.0 * lane_index / HD)
    return row_index.astype(jnp.float32)[:, None] * frequency[None, :]


def rotate(head_values, angles):
    half_width = head_values.shape[-1] // 2
    first_half = head_values[..., :half_width]
    second_half = head_values[..., half_width:]
    cosine = jnp.cos(angles)[:, None, :]
    sine_part = jnp.sin(angles)[:, None, :]
    return jnp.concatenate(
        [
            first_half * cosine - second_half * sine_part,
            second_half * cosine + first_half * sine_part,
        ],
        axis=-1,
    )


def normalize(routed, norm_gain):
    wide_rows = routed.astype(jnp.float32)
    inv_rms = lax.rsqrt(jnp.mean(wide_rows * wide_rows, axis=1, keepdims=True) + NORM_EPS)
    return (wide_rows * inv_rms * norm_gain[None, :]).astype(jnp.bfloat16)


def local(hidden_rows, destination, doc_ids, norm_gain, w_query, w_key, w_value, w_out):
    owners = lax.axis_size("dp")
    my_index = lax.axis_index("dp")
    tok_dev, columns = hidden_rows.shape
    capacity = 2 * tok_dev // owners
    target = destination // tok_dev
    owner_ids = jnp.arange(owners, dtype=jnp.int32)
    one_hot = (target[:, None] == owner_ids[None, :]).astype(jnp.int32)
    slot_rank = jnp.sum((jnp.cumsum(one_hot, axis=0) - 1) * one_hot, axis=1)
    flat_slot = target * capacity + slot_rank
    outgoing = (
        jnp.zeros((owners * capacity, columns), hidden_rows.dtype).at[flat_slot].set(hidden_rows)
    )
    places = (
        jnp.full((owners * capacity,), tok_dev, jnp.int32).at[flat_slot].set(destination % tok_dev)
    )
    arrived, arrived_rows = (
        lax.all_to_all(
            outgoing.reshape(owners, capacity, columns),
            "dp",
            split_axis=0,
            concat_axis=0,
            tiled=True,
        ),
        lax.all_to_all(
            places.reshape(owners, capacity), "dp", split_axis=0, concat_axis=0, tiled=True
        ),
    )
    arrived_rows = arrived_rows.reshape(-1)
    routed_part = (
        jnp.zeros((tok_dev, columns), hidden_rows.dtype)
        .at[arrived_rows]
        .set(arrived.reshape(-1, columns), mode="drop")
    )
    routed = lax.all_gather(routed_part, "mp", axis=1, tiled=True)
    normed = normalize(routed, norm_gain)
    heads_dev = w_query.shape[1] // HD
    kv_dev = w_key.shape[1] // HD
    group_size = heads_dev // kv_dev
    query_rows = my_index * tok_dev + jnp.arange(tok_dev, dtype=jnp.int32)
    angles = rope_angles(query_rows)
    queries = jnp.dot(normed, w_query, preferred_element_type=jnp.float32).reshape(
        tok_dev, heads_dev, HD
    )
    queries = rotate(queries, angles).astype(jnp.bfloat16).reshape(tok_dev, kv_dev, group_size, HD)
    keys_own = jnp.dot(normed, w_key, preferred_element_type=jnp.float32).reshape(
        tok_dev, kv_dev, HD
    )
    keys_own = rotate(keys_own, angles).astype(jnp.bfloat16)
    values_own = (
        jnp.dot(normed, w_value, preferred_element_type=jnp.float32)
        .astype(jnp.bfloat16)
        .reshape(tok_dev, kv_dev, HD)
    )
    score_scale = HD ** (-0.5)
    query_first = doc_ids[0]
    query_last = doc_ids[tok_dev - 1]
    last_row = query_rows[tok_dev - 1]

    def attend_block(soft_state, block_in):
        keys_blk, values_blk, ids_blk, key_rows = block_in
        row_best, row_total, weighted = soft_state
        scores = (
            jnp.einsum("qgrd,kgd->grqk", queries, keys_blk, preferred_element_type=jnp.float32)
            * score_scale
        )
        allowed = (doc_ids[:, None] == ids_blk[None, :]) & (
            key_rows[None, :] <= query_rows[:, None]
        )
        scores = jnp.where(allowed[None, None], scores, -jnp.inf)
        new_best = jnp.maximum(row_best, jnp.max(scores, axis=-1))
        rescale = jnp.exp(row_best - new_best)
        exp_scores = jnp.exp(scores - new_best[..., None])
        row_total = row_total * rescale + jnp.sum(exp_scores, axis=-1)
        weighted = weighted * rescale[..., None] + jnp.einsum(
            "grqk,kgd->grqd",
            exp_scores.astype(jnp.bfloat16),
            values_blk,
            preferred_element_type=jnp.float32,
        )
        return ((new_best, row_total, weighted), None)

    start_state = (
        jnp.full((kv_dev, group_size, tok_dev), NEG_START, jnp.float32),
        jnp.zeros((kv_dev, group_size, tok_dev), jnp.float32),
        jnp.zeros((kv_dev, group_size, tok_dev, HD), jnp.float32),
    )
    first_row = jnp.int32(0)
    keys_piece = lax.all_gather(keys_own, "dp", axis=0, tiled=True)
    values_piece = lax.all_gather(values_own, "dp", axis=0, tiled=True)
    ids_piece = lax.all_gather(doc_ids, "dp", axis=0, tiled=True)
    key_count = keys_piece.shape[0]
    block_len = math.gcd(key_count, key_block)
    step_count = key_count // block_len
    relevant = (
        (first_row >= 0)
        & (first_row <= last_row)
        & (ids_piece[key_count - 1] >= query_first)
        & (ids_piece[0] <= query_last)
    )

    def run_piece(state_in):
        rows_piece = jnp.arange(key_count, dtype=jnp.int32)
        blocks_in = (
            keys_piece.reshape(step_count, block_len, kv_dev, HD),
            values_piece.reshape(step_count, block_len, kv_dev, HD),
            ids_piece.reshape(step_count, block_len),
            rows_piece.reshape(step_count, block_len),
        )
        return lax.scan(attend_block, state_in, blocks_in)[0]

    def keep_state(state_in):
        return state_in

    soft_state = lax.cond(relevant, run_piece, keep_state, start_state)
    row_best, row_total, weighted = soft_state
    context = (
        jnp.transpose(weighted / row_total[..., None], (2, 0, 1, 3))
        .reshape(tok_dev, heads_dev * HD)
        .astype(jnp.bfloat16)
    )
    partial_out = jnp.dot(context, w_out, preferred_element_type=jnp.float32)
    summed = lax.psum_scatter(partial_out, "mp", scatter_dimension=1, tiled=True)
    attended = (routed_part.astype(jnp.float32) + summed).astype(jnp.bfloat16)
    backward = attended[jnp.minimum(arrived_rows, tok_dev - 1)].reshape(owners, capacity, columns)
    returned = lax.all_to_all(backward, "dp", split_axis=0, concat_axis=0, tiled=True)
    return returned.reshape(owners * capacity, columns)[flat_slot]


def solution(mesh):
    in_specs = (
        P("dp", "mp"),
        P("dp"),
        P("dp"),
        P(),
        P(None, "mp"),
        P(None, "mp"),
        P(None, "mp"),
        P("mp", None),
    )
    out_specs = P("dp", "mp")
    return jax.shard_map(local, mesh=mesh, in_specs=in_specs, out_specs=out_specs, check_vma=False)
```

profile of v0, /device:TPU:1, one launch (start us, length us, event | category | flops | bytes accessed | tf_op | source)
XLA Modules:
  0.0 689.3 jit_solution(14763836879183577752)
XLA Ops:
  12.0 9.6 %all-to-all-start = ((s32[32,1,32]{2,1,0:T(1,128)}), s32[32,1,32]{2,1,0:T(1,128)S(1)}, u32[]{:S(2)}, u32[]{:S(2)}) async-start(s32[32,1,32]{2,1,0:T(1,128)} %all_to_all.12), calls=%async_computation | async-start | bytes 32768 | tf_op jit(solution)/shard_map/all_to_all | solution.py:65
  21.6 4.8 scatter_custom_fusion.1
  28.5 5.3 all-to-all-start.1
  35.2 26.9 %all-to-all-done.1 = bf16[32,32,1024]{2,1,0:T(8,128)(2,1)S(1)} async-done(((bf16[32,32,1024]{2,1,0:T(8,128)(2,1)}), bf16[32,32,1024]{2,1,0:T(8,128)(2,1)S(1)}, u32[]{:S(2)}, u32[]{:S(2)}) %all-to-all-start.1) | async-done | bytes 2097184 | tf_op jit(solution)/shard_map/all_to_all | solution.py:58
  62.1 6.2 scatter_custom_fusion.2
  68.5 45.7 %all-gather.6.cloned.1.call-done = bf16[512,4096]{1,0:T(8,128)(2,1)} async-done(((bf16[512,1024]{1,0:T(8,128)(2,1)}), bf16[512,4096]{1,0:T(8,128)(2,1)}) %all-gather.6.cloned.1.call-update) | async-done | bytes 4194320 | tf_op jit(solution)/shard_map/all_gather | solution.py:75
  120.8 4.2 convolution_convert_fusion
  125.6 24.9 %all-gather.1 = s32[32,1,512]{2,1,0:T(1,128)S(1)} all-gather(s32[1,1,512]{2,1,0:T(1,128)S(1)} %bitcast.137), channel_id=1, replica_groups=mesh['dp'=32,'mp'=4] {'dp'}, dimensions={0}, use_global_device_ids=true | all-gather | bytes 67584 | tf_op jit(solution)/shard_map/all_gather | solution.py:131
  156.4 6.2 fusion.48
  166.8 4.1 all-gather.8.cloned.1.call-done
  170.9 48.1 %all-gather.10.cloned.1.call-done = bf16[16384,128]{1,0:T(8,128)(2,1)} async-done(((bf16[512,128]{1,0:T(8,128)(2,1)}), bf16[16384,128]{1,0:T(8,128)(2,1)}) %all-gather.10.cloned.1.call-update) | async-done | bytes 4194320 | tf_op jit(solution)/shard_map/all_gather | solution.py:130
  219.0 329.5 %conditional.1 = (f32[1,4,512]{2,1,0:T(4,128)}, f32[1,4,512,128]{2,3,1,0:T(8,128)S(1)}) conditional(s32[]{:T(128)} %bitcast.9, () %tuple.17, (bf16[16384,1,128]{0,2,1:T(8,128)(2,1)}, bf16[16384,1,128]{2,0,1:T(8,128)(2,1)}, s32[16384]{0:T(1024)S(1)}, s32[512]{0:T(512)S(1)}, s32[512]{0:T(512)S(1)}, ...), branch_computations={%region_7.8_spmd, %region_8.13_spmd} | conditional | flops 550023168 | bytes 48317764 | solution.py:155
  219.0 6.4 copy.23
  225.4 320.3 %while.14 = (s32[]{:T(128)}, f32[1,4,512]{2,1,0:T(4,128)S(1)}, f32[1,4,512]{2,1,0:T(4,128)}, f32[1,4,512,128]{3,2,1,0:T(8,128)S(1)}, s32[512]{0:T(512)S(1)}, /*i...) while((s32[]{:T(128)}, f32[1,4,512]{2,1,0:T(4,128)S(1)}, ...), condition=%wide.region_12.12_spmd.clone, body=%wide.region_9.11_spmd.clone.sunk | while | flops 549990400 | bytes 33440936 | solution.py:150
  248.8 3.8 fusion.72
  268.8 3.8 fusion.72
  278.9 3.8 fusion.72
  298.9 3.8 fusion.72
  309.0 3.8 fusion.72
  549.4 7.8 %fusion.55 = f32[512,4096]{1,0:T(8,128)} fusion(bf16[512,512]{0,1:T(8,128)(2,1)S(1)} %bitcast.130, bf16[512,4096]{1,0:T(8,128)(2,1)} %param.19), kind=kOutput, calls=%fused_computation.97 | convolution fusion | flops 2147483648 | bytes 13107200 | tf_op jit(solution)/shard_map/dot_general | solution.py:162
  557.2 79.5 %reduce-scatter.2.cloned.1.call-done = f32[512,1024]{1,0:T(8,128)} async-done(((f32[512,4096]{1,0:T(8,128)}), f32[512,1024]{1,0:T(8,128)}) %reduce-scatter.2.cloned.1.call-update) | async-done | bytes 2097168 | tf_op jit(solution)/shard_map/reduce_scatter | solution.py:163
  638.7 5.3 gather_fusion
  644.0 7.7 %all-to-all-start.2 = ((bf16[32,32,1024]{2,1,0:T(8,128)(2,1)}), bf16[32,32,1024]{2,1,0:T(8,128)(2,1)S(1)}, u32[]{:S(2)}, u32[]{:S(2)}) async-start(bf16[32,32,1024]{2,1,0:T(8,128)(2,1)} %bitcast.126), calls=%async_computation.3 | async-start | bytes 4194304 | tf_op jit(solution)/shard_map/all_to_all | solution.py:166
  651.7 28.3 %all-to-all-done.2 = bf16[32,32,1024]{2,1,0:T(8,128)(2,1)S(1)} async-done(((bf16[32,32,1024]{2,1,0:T(8,128)(2,1)}), bf16[32,32,1024]{2,1,0:T(8,128)(2,1)S(1)}, u32[]{:S(2)}, u32[]{:S(2)}) %all-to-all-start.2) | async-done | bytes 2097184 | tf_op jit(solution)/shard_map/all_to_all | solution.py:166
  (380 shorter events, 331.6 us)
Async XLA Ops:
  6.5 110.9 %copy-start = (bf16[4096,128]{1,0:T(8,128)(2,1)S(1)}, bf16[4096,128]{1,0:T(8,128)(2,1)}, u32[]{:S(2)}) copy-start(bf16[4096,128]{1,0:T(8,128)(2,1)} %param.17) | copy-start | bytes 3145732
  12.0 16.5 %all-to-all-start = ((s32[32,1,32]{2,1,0:T(1,128)}), s32[32,1,32]{2,1,0:T(1,128)S(1)}, u32[]{:S(2)}, u32[]{:S(2)}) async-start(s32[32,1,32]{2,1,0:T(1,128)} %all_to_all.12), calls=%async_computation | async-start | bytes 32768 | tf_op jit(solution)/shard_map/all_to_all | solution.py:65
  28.5 33.6 %all-to-all-start.1 = ((bf16[32,32,1024]{2,1,0:T(8,128)(2,1)}), bf16[32,32,1024]{2,1,0:T(8,128)(2,1)S(1)}, u32[]{:S(2)}, u32[]{:S(2)}) async-start(bf16[32,32,1024]{2,1,0:T(8,128)(2,1)} %bitcast.5), calls=%async_computation.1 | async-start | bytes 4194304 | tf_op jit(solution)/shard_map/all_to_all | solution.py:58
  33.9 83.6 %copy-start.7 = (f32[4096]{0:T(1024)S(1)}, f32[4096]{0:T(1024)}, u32[]{:S(2)}) copy-start(f32[4096]{0:T(1024)} %param.15) | copy-start | bytes 49156
  33.9 80.3 %all-gather.6.cloned.1.call-start = ((), (), s32[]{:S(2)}) async-start(), calls=%async_computation.4 | async-start | bytes 5242880 | tf_op jit(solution)/shard_map/all_gather | solution.py:75
  68.4 102.5 %all-gather.8.cloned.1.call-start = ((), (), s32[]{:S(2)}) async-start(), calls=%async_computation.5 | async-start | bytes 4325376 | tf_op jit(solution)/shard_map/all_gather | solution.py:129
  120.5 5.1 copy-start.5
  120.5 98.5 %all-gather.10.cloned.1.call-start = ((), (), s32[]{:S(2)}) async-start(), calls=%async_computation.7 | async-start | bytes 4325376 | tf_op jit(solution)/shard_map/all_gather | solution.py:130
  124.9 511.8 %reduce-scatter.2.cloned.1.call-start = ((), (), s32[]{:S(2)}) async-start(), calls=%async_computation.6 | async-start | bytes 10485760 | tf_op jit(solution)/shard_map/reduce_scatter | solution.py:163
  248.8 3.8 copy-start.1
  258.8 3.8 copy-start.1
  268.8 3.8 copy-start.1
  288.9 3.8 copy-start.1
  298.9 3.8 copy-start.1
  319.0 3.8 copy-start.1
  329.0 3.8 copy-start.1
  339.0 3.8 copy-start.1
  349.1 3.8 copy-start.1
  359.1 3.8 copy-start.1
  369.1 3.8 copy-start.1
  379.1 3.8 copy-start.1
  389.2 3.8 copy-start.1
  557.2 79.6 %copy-start.2 = (bf16[512,1024]{1,0:T(8,128)(2,1)S(1)}, bf16[512,1024]{1,0:T(8,128)(2,1)}, u32[]{:S(2)}) copy-start(bf16[512,1024]{1,0:T(8,128)(2,1)} %scatter_custom_fusion.2) | copy-start | bytes 3145732
  644.0 36.0 %all-to-all-start.2 = ((bf16[32,32,1024]{2,1,0:T(8,128)(2,1)}), bf16[32,32,1024]{2,1,0:T(8,128)(2,1)S(1)}, u32[]{:S(2)}, u32[]{:S(2)}) async-start(bf16[32,32,1024]{2,1,0:T(8,128)(2,1)} %bitcast.126), calls=%async_computation.3 | async-start | bytes 4194304 | tf_op jit(solution)/shard_map/all_to_all | solution.py:166
  (22 other events, 80.6 us)
Sparse Core Ops, SparseCore 0:
  68.5 45.6 all-gather.5
  120.6 50.2 all-gather.7
  173.2 45.8 all-gather.9
  557.3 79.3 reduce-scatter.1
where the time goes:
time: 692 us; the launch traced here: 689 us
  matrix products  259 us (37%)
  waiting for transfers between devices  235 us (34%)
  other arithmetic  93.1 us (13%)
  local copies, waits for them, and re-layouts  37.1 us (5%)
  blocking collectives  24.9 us (4%)
  starting transfers between devices  22.9 us (3%)
  between operations  16.3 us (2%)
    dot_general x32, matrix products, attend_block(): jnp.einsum('grqk,kgd->grqd', exp_scores.astype(jnp.bfloat16), values_blk,...  122 us
    dot_general x32, matrix products, attend_block(): jnp.einsum('qgrd,kgd->grqk', queries, keys_blk, preferred_element_type=jn...  117 us
    reduce_scatter x1, waiting for transfers between devices, local(): lax.psum_scatter(partial_out, 'mp', scatter_dimension=1, tiled=True)  79.5 us
    all_gather x1, waiting for transfers between devices, local(): values_piece = lax.all_gather(values_own, 'dp', axis=0, tiled=True)  48.1 us
    all_gather x1, waiting for transfers between devices, local(): routed = lax.all_gather(routed_part, 'mp', axis=1, tiled=True)  45.7 us
    add x32, other arithmetic, attend_block(): row_total = row_total * rescale + jnp.sum(exp_scores, axis=-1)  41.2 us
    reduce_sum x32, other arithmetic, attend_block(): row_total = row_total * rescale + jnp.sum(exp_scores, axis=-1)  29.3 us
    all_to_all x1, waiting for transfers between devices, local(): lax.all_to_all(backward, 'dp', split_axis=0, concat_axis=0, tiled=True)  28.3 us
  transfers between devices with their start and end apart: 7, of which 7 were waited for; matrix products, arithmetic and copies ran while one was open for 4% of the time, Pallas kernels for 0%

commit v1 on v0

--- a/solution.py
+++ b/solution.py
@@ -127,7 +127,9 @@
     )
     first_row = jnp.int32(0)
     keys_piece = lax.all_gather(keys_own, "dp", axis=0, tiled=True)
-    values_piece = lax.all_gather(values_own, "dp", axis=0, tiled=True)
+    values_piece = jnp.concatenate(
+        lax.all_to_all(jnp.stack([values_own] * lax.axis_size("dp")), "dp", 0, 0), axis=0
+    )
     ids_piece = lax.all_gather(doc_ids, "dp", axis=0, tiled=True)
     key_count = keys_piece.shape[0]
     block_len = math.gcd(key_count, key_block)

time: 692 us -> 692 us (level)
  waiting for transfers between devices: 235 us -> 182 us
  blocking collectives: 24.9 us -> 73.2 us
  starting transfers between devices: 22.9 us -> 30.8 us
    all_gather x1, blocking collectives: 24.9 us -> 73.2 us  [local(): ids_piece = lax.all_gather(doc_ids, 'dp', axis=0, tiled=True)]
    all_gather x1 -> x0, waiting for transfers between devices: 48.1 us -> none  [local(): values_piece = lax.all_gather(values_own, 'dp', axis=0, tiled=True)]
    all_to_all x0 -> x1, starting transfers between devices: none -> 7.93 us  [local(): lax.all_to_all(jnp.stack([values_own] * lax.axis_size('dp')), 'dp', 0, 0)]
  transfers between devices with their start and end apart: 7 -> 7, of which waited for: 7 -> 5; matrix products, arithmetic and copies ran while one was open for 4% -> 3% of each run, Pallas kernels for 0% -> 0%
where the time goes in v1:
time: 692 us; the launch traced here: 689 us
  matrix products  258 us (37%)
  waiting for transfers between devices  182 us (26%)
  other arithmetic  91.3 us (13%)
  blocking collectives  73.2 us (11%)
  local copies, waits for them, and re-layouts  35.9 us (5%)
  starting transfers between devices  30.8 us (4%)
  between operations  16.4 us (2%)
    dot_general x32, matrix products, attend_block(): jnp.einsum('grqk,kgd->grqd', exp_scores.astype(jnp.bfloat16), values_blk,...  122 us
    dot_general x32, matrix products, attend_block(): jnp.einsum('qgrd,kgd->grqk', queries, keys_blk, preferred_element_type=jn...  117 us
    reduce_scatter x1, waiting for transfers between devices, local(): lax.psum_scatter(partial_out, 'mp', scatter_dimension=1, tiled=True)  78.9 us
    all_gather x1, blocking collectives, local(): ids_piece = lax.all_gather(doc_ids, 'dp', axis=0, tiled=True)  73.2 us
    all_gather x1, waiting for transfers between devices, local(): routed = lax.all_gather(routed_part, 'mp', axis=1, tiled=True)  45.5 us
    add x32, other arithmetic, attend_block(): row_total = row_total * rescale + jnp.sum(exp_scores, axis=-1)  41.2 us
    reduce_sum x32, other arithmetic, attend_block(): row_total = row_total * rescale + jnp.sum(exp_scores, axis=-1)  29.3 us
    all_to_all x1, waiting for transfers between devices, local(): lax.all_to_all(backward, 'dp', split_axis=0, concat_axis=0, tiled=True)  28.3 us
  transfers between devices with their start and end apart: 7, of which 5 were waited for; matrix products, arithmetic and copies ran while one was open for 3% of the time, Pallas kernels for 0%

profile of v1, /device:TPU:1, one launch (start us, length us, event | category | flops | bytes accessed | tf_op | source)
XLA Modules:
  0.0 688.9 jit_solution(15318927313271304495)
XLA Ops:
  12.0 9.6 %all-to-all-start = ((s32[32,1,32]{2,1,0:T(1,128)}), s32[32,1,32]{2,1,0:T(1,128)S(1)}, u32[]{:S(2)}, u32[]{:S(2)}) async-start(s32[32,1,32]{2,1,0:T(1,128)} %all_to_all.15), calls=%async_computation | async-start | bytes 32768 | tf_op jit(solution)/shard_map/all_to_all | solution.py:65
  21.6 4.8 scatter_custom_fusion.1
  28.5 5.3 all-to-all-start.1
  35.2 26.9 %all-to-all-done.1 = bf16[32,32,1024]{2,1,0:T(8,128)(2,1)S(1)} async-done(((bf16[32,32,1024]{2,1,0:T(8,128)(2,1)}), bf16[32,32,1024]{2,1,0:T(8,128)(2,1)S(1)}, u32[]{:S(2)}, u32[]{:S(2)}) %all-to-all-start.1) | async-done | bytes 2097184 | tf_op jit(solution)/shard_map/all_to_all | solution.py:58
  62.2 6.2 scatter_custom_fusion.2
  68.7 45.5 %all-gather.4.cloned.1.call-done = bf16[512,4096]{1,0:T(8,128)(2,1)} async-done(((bf16[512,1024]{1,0:T(8,128)(2,1)}), bf16[512,4096]{1,0:T(8,128)(2,1)}) %all-gather.4.cloned.1.call-update) | async-done | bytes 4194320 | tf_op jit(solution)/shard_map/all_gather | solution.py:75
  126.9 7.9 %all-to-all-start.2 = ((bf16[32,512,1,128]{3,1,2,0:T(8,128)(2,1)}), bf16[32,512,1,128]{3,1,2,0:T(8,128)(2,1)}, u32[]{:S(2)}, u32[]{:S(2)}) async-start(bf16[32,512,1,128]{3,1,2,0:T(8,128)(2,1)} %stack.3), calls=%async_computation.2 | async-start | bytes 8388608 | tf_op jit(solution)/shard_map/all_to_all | solution.py:131
  135.5 73.2 %all-gather = s32[32,1,512]{2,1,0:T(1,128)S(1)} all-gather(s32[1,1,512]{2,1,0:T(1,128)S(1)} %bitcast.135), channel_id=1, replica_groups=mesh['dp'=32,'mp'=4] {'dp'}, dimensions={0}, use_global_device_ids=true | all-gather | bytes 67584 | tf_op jit(solution)/shard_map/all_gather | solution.py:133
  213.9 5.9 fusion.49
  221.3 327.5 %conditional.1 = (f32[1,4,512]{2,1,0:T(4,128)}, f32[1,4,512,128]{2,3,1,0:T(8,128)S(1)}) conditional(s32[]{:T(128)} %bitcast.8, () %tuple.17, (bf16[16384,1,128]{0,2,1:T(8,128)(2,1)}, s32[16384]{0:T(1024)S(1)}, s32[512]{0:T(512)S(1)}, s32[512]{0:T(512)S(1)}, bf16[512,1,4,128]{3,0,2,1:T(8,128)(2,1)S(1)}, ...), branch_computations={%region_7.8_spmd, %region_8.13_spmd} | conditional | flops 550023168 | bytes 44123432 | solution.py:157
  221.5 6.4 copy.23
  227.9 320.5 %while.14 = (s32[]{:T(128)}, f32[1,4,512]{2,1,0:T(4,128)S(1)}, f32[1,4,512]{2,1,0:T(4,128)}, f32[1,4,512,128]{3,2,1,0:T(8,128)S(1)}, s32[512]{0:T(512)S(1)}, /*i...) while((s32[]{:T(128)}, f32[1,4,512]{2,1,0:T(4,128)S(1)}, ...), condition=%wide.region_12.12_spmd.clone, body=%wide.region_9.11_spmd.clone.sunk | while | flops 549990400 | bytes 33440936 | solution.py:152
  231.9 3.8 fusion.72
  241.3 3.8 fusion.72
  261.4 3.8 fusion.72
  281.4 3.8 fusion.72
  301.5 3.8 fusion.72
  321.6 3.8 fusion.72
  522.3 3.8 fusion.72
  549.6 7.8 %fusion.55 = f32[512,4096]{1,0:T(8,128)} fusion(bf16[512,512]{0,1:T(8,128)(2,1)S(1)} %bitcast.128, bf16[512,4096]{1,0:T(8,128)(2,1)} %param.19), kind=kOutput, calls=%fused_computation.97 | convolution fusion | flops 2147483648 | bytes 13107200 | tf_op jit(solution)/shard_map/dot_general | solution.py:164
  557.5 78.9 %reduce-scatter.2.cloned.1.call-done = f32[512,1024]{1,0:T(8,128)} async-done(((f32[512,4096]{1,0:T(8,128)}), f32[512,1024]{1,0:T(8,128)}) %reduce-scatter.2.cloned.1.call-update) | async-done | bytes 2097168 | tf_op jit(solution)/shard_map/reduce_scatter | solution.py:165
  638.3 5.3 gather_fusion
  643.7 7.6 %all-to-all-start.3 = ((bf16[32,32,1024]{2,1,0:T(8,128)(2,1)}), bf16[32,32,1024]{2,1,0:T(8,128)(2,1)S(1)}, u32[]{:S(2)}, u32[]{:S(2)}) async-start(bf16[32,32,1024]{2,1,0:T(8,128)(2,1)} %bitcast.124), calls=%async_computation.4 | async-start | bytes 4194304 | tf_op jit(solution)/shard_map/all_to_all | solution.py:168
  651.3 28.3 %all-to-all-done.3 = bf16[32,32,1024]{2,1,0:T(8,128)(2,1)S(1)} async-done(((bf16[32,32,1024]{2,1,0:T(8,128)(2,1)}), bf16[32,32,1024]{2,1,0:T(8,128)(2,1)S(1)}, u32[]{:S(2)}, u32[]{:S(2)}) %all-to-all-start.3) | async-done | bytes 2097184 | tf_op jit(solution)/shard_map/all_to_all | solution.py:168
  (380 shorter events, 324.7 us)
Async XLA Ops:
  6.5 110.9 %copy-start = (bf16[4096,128]{1,0:T(8,128)(2,1)S(1)}, bf16[4096,128]{1,0:T(8,128)(2,1)}, u32[]{:S(2)}) copy-start(bf16[4096,128]{1,0:T(8,128)(2,1)} %param.17) | copy-start | bytes 3145732
  12.0 16.5 %all-to-all-start = ((s32[32,1,32]{2,1,0:T(1,128)}), s32[32,1,32]{2,1,0:T(1,128)S(1)}, u32[]{:S(2)}, u32[]{:S(2)}) async-start(s32[32,1,32]{2,1,0:T(1,128)} %all_to_all.15), calls=%async_computation | async-start | bytes 32768 | tf_op jit(solution)/shard_map/all_to_all | solution.py:65
  28.5 33.7 %all-to-all-start.1 = ((bf16[32,32,1024]{2,1,0:T(8,128)(2,1)}), bf16[32,32,1024]{2,1,0:T(8,128)(2,1)S(1)}, u32[]{:S(2)}, u32[]{:S(2)}) async-start(bf16[32,32,1024]{2,1,0:T(8,128)(2,1)} %bitcast.4), calls=%async_computation.1 | async-start | bytes 4194304 | tf_op jit(solution)/shard_map/all_to_all | solution.py:58
  33.9 83.6 %copy-start.7 = (f32[4096]{0:T(1024)S(1)}, f32[4096]{0:T(1024)}, u32[]{:S(2)}) copy-start(f32[4096]{0:T(1024)} %param.15) | copy-start | bytes 49156
  33.9 80.3 %all-gather.4.cloned.1.call-start = ((), (), s32[]{:S(2)}) async-start(), calls=%async_computation.5 | async-start | bytes 5242880 | tf_op jit(solution)/shard_map/all_gather | solution.py:75
  68.4 152.9 %all-gather.6.cloned.1.call-start = ((), (), s32[]{:S(2)}) async-start(), calls=%async_computation.6 | async-start | bytes 4325376 | tf_op jit(solution)/shard_map/all_gather | solution.py:129
  126.9 8.6 %copy-start.5 = (s32[512]{0:T(512)S(1)}, s32[512]{0:T(512)}, u32[]{:S(2)}) copy-start(s32[512]{0:T(512)} %param.14) | copy-start | bytes 6148
  126.9 94.3 %all-to-all-start.2 = ((bf16[32,512,1,128]{3,1,2,0:T(8,128)(2,1)}), bf16[32,512,1,128]{3,1,2,0:T(8,128)(2,1)}, u32[]{:S(2)}, u32[]{:S(2)}) async-start(bf16[32,512,1,128]{3,1,2,0:T(8,128)(2,1)} %stack.3), calls=%async_computation.2 | async-start | bytes 8388608 | tf_op jit(solution)/shard_map/all_to_all | solution.py:131
  134.9 501.5 %reduce-scatter.2.cloned.1.call-start = ((), (), s32[]{:S(2)}) async-start(), calls=%async_computation.7 | async-start | bytes 10485760 | tf_op jit(solution)/shard_map/reduce_scatter | solution.py:165
  231.9 3.8 copy-start.2
  241.3 3.8 copy-start.2
  261.3 3.8 copy-start.2
  281.4 3.8 copy-start.2
  301.5 3.8 copy-start.2
  321.6 3.8 copy-start.2
  341.6 3.8 copy-start.2
  361.7 3.8 copy-start.2
  381.8 3.8 copy-start.2
  401.9 3.8 copy-start.2
  421.9 3.8 copy-start.2
  442.0 3.8 copy-start.2
  462.1 3.8 copy-start.2
  557.4 78.9 %copy-start.3 = (bf16[512,1024]{1,0:T(8,128)(2,1)S(1)}, bf16[512,1024]{1,0:T(8,128)(2,1)}, u32[]{:S(2)}) copy-start(bf16[512,1024]{1,0:T(8,128)(2,1)} %scatter_custom_fusion.2) | copy-start | bytes 3145732
  643.7 35.9 %all-to-all-start.3 = ((bf16[32,32,1024]{2,1,0:T(8,128)(2,1)}), bf16[32,32,1024]{2,1,0:T(8,128)(2,1)S(1)}, u32[]{:S(2)}, u32[]{:S(2)}) async-start(bf16[32,32,1024]{2,1,0:T(8,128)(2,1)} %bitcast.124), calls=%async_computation.4 | async-start | bytes 4194304 | tf_op jit(solution)/shard_map/all_to_all | solution.py:168
  (22 other events, 82.1 us)
Sparse Core Ops, SparseCore 0:
  68.5 45.6 all-gather.3
  120.6 80.5 all-gather.5
  557.6 78.7 reduce-scatter.1
